TPU v7x, 512 devices: a whole 4x8x8 slice. The times are simulated.
512 devices in a mesh: grp: 8 (over y_lo, core), own: 64 (over x, y_hi, z).
Axes of the slice: x: 4, y: 8 (y_hi: 2, y_lo: 4; y = y_hi * 4 + y_lo), z: 8, core: 2. Of those that a mesh axis runs over, the one named last changes fastest.
Arguments:
- activations: bfloat16 [65536, 1024], P(('grp', 'own'))
- out_grads: bfloat16 [65536, 1024], P(('grp', 'own')), may hold values from -0.01953125 to 0.01953125
- master: float32 [1024, 1024], P('own'), may hold values from -6 to 6
- moment: float32 [1024, 1024], P('own'), may hold values from 0.05 to 5
- left_root: bfloat16 [1024, 1024], P('own'), may hold values from -0.25 to 2.25, as said below
- right_root: bfloat16 [1024, 1024], P('own'), may hold values from -0.25 to 2.25, as said below
- stats_in: float32 [256, 16, 1024], P('own'), may hold values from -6 to 6
- tile_slot: int32 [128], replicated, may hold values from 0 to 255, as said below
Outputs:
- master_out: float32 [1024, 1024], P('own')
- moment_out: float32 [1024, 1024], P('own')
- stats_out: float32 [256, 16, 1024], P('own')
- weights: bfloat16 [1024, 1024], replicated
Inputs may be any that keep to these rules, and one draw needn't show every extreme that they name: `tile_slot`: distinct slot numbers; slot s belongs to owner s // 4; some owner holds 4 tiles. `left_root`: symmetric. `right_root`: symmetric.
All inputs are finite; a program needn't handle non-finite values.
Results may differ from a plain program's by a relative error of at most 0.005.
Values may be sent and summed in bfloat16 or wider, within the bound.
No kernel may reach another device: no remote copies, remote signals or barrier semaphores. Data moves between devices by JAX's collectives and lax.ppermute only.
A program may use at most 64 MiB of HBM per device.

v0:
```python
import jax
import jax.numpy as jnp
from jax import lax
from jax.sharding import Mesh
from jax.sharding import PartitionSpec as P

stat_decay = 0.9
moment_decay = 0.95
learn_rate = 0.3
adam_eps = 1e-08
norm_eps = 1e-06

GRP = ("yl", "c")
OWN = ("x", "yh", "z")
SUB_SIZES = (4, 2, 4, 2, 8)


def split3(value):
    hi = lax.reduce_precision(value, exponent_bits=8, mantissa_bits=7)
    rest = value - hi
    mid = lax.reduce_precision(rest, exponent_bits=8, mantissa_bits=7)
    lo = lax.reduce_precision(rest - mid, exponent_bits=8, mantissa_bits=7)
    return jnp.stack([hi, mid, lo])


def gather_own_rows(block):
    rows = block.shape[0]
    out = block
    for axis in ("yh", "x", "z"):
        out = lax.all_gather(out, axis, axis=0, tiled=True)
    out = out.reshape(SUB_SIZES[4], SUB_SIZES[2], SUB_SIZES[3], rows, block.shape[1])
    out = jnp.transpose(out, (1, 2, 0, 3, 4))
    return out.reshape(-1, block.shape[1])


def join_cores(parts, cores):
    both = lax.all_to_all(jnp.broadcast_to(parts[None], (cores,) + parts.shape), "c", 0, 0, tiled=True)
    return jnp.transpose(both, (1, 0, 2, 3)).reshape(-1, parts.shape[-1])


def local(activations, out_grads, master, moment, left_root, right_root, stats_in, tile_slot):
    owner_rows = master.shape[0]
    block_size = master.shape[1]
    owners = block_size // owner_rows
    capacity = stats_in.shape[0]
    tile_rows = stats_in.shape[1]
    tile_count = tile_slot.shape[0]
    owner_index = lax.axis_index(OWN)
    grp_size = SUB_SIZES[0] * SUB_SIZES[1]


    partial = lax.dot_general(
        activations, out_grads, (((0,), (0,)), ((), ())), preferred_element_type=jnp.float32
    )
    cores = SUB_SIZES[1]
    part_rows = owner_rows // cores
    halves = jnp.transpose(partial.reshape(owners, cores, part_rows, block_size), (1, 0, 2, 3))
    chip_sum = jnp.sum(lax.all_to_all(halves, "c", 0, 0, tiled=True), axis=0)
    pieces = lax.all_to_all(chip_sum, OWN, 0, 0, tiled=True)
    own_sum = jnp.sum(pieces, axis=0)
    copies = jnp.broadcast_to(own_sum[None], (grp_size, part_rows, block_size))
    got_grp = lax.all_to_all(copies, GRP, 0, 0, tiled=True).reshape(
        SUB_SIZES[0], cores, part_rows, block_size
    )
    grad_rows = jnp.sum(got_grp, axis=0).reshape(owner_rows, block_size)

    moment_out = moment_decay * moment + (1.0 - moment_decay) * grad_rows * grad_rows
    adam_dir = grad_rows / (jnp.sqrt(moment_out) + adam_eps)
    adam_part = split3(jnp.sum(adam_dir * adam_dir))

    extra = jnp.zeros((1, block_size), jnp.float32).at[0, :3].set(adam_part)
    core = lax.axis_index("c")
    my_part = lax.dynamic_slice_in_dim(grad_rows, core * part_rows, part_rows, 0)
    root_part = lax.dynamic_slice_in_dim(right_root, core * part_rows, part_rows, 0)
    payload = jnp.concatenate(
        [my_part.astype(jnp.bfloat16), extra.astype(jnp.bfloat16), root_part], axis=0
    )
    sent = jnp.broadcast_to(payload[None], (owners,) + payload.shape)
    got = lax.all_to_all(sent, OWN, 0, 0, tiled=True)
    adam_sum = jnp.sum(got[:, part_rows, :3].astype(jnp.float32))
    mine = jnp.concatenate([got[:, :part_rows, :], got[:, part_rows + 1 :, :]], axis=1)
    both = lax.all_to_all(jnp.broadcast_to(mine[None], (cores,) + mine.shape), "c", 0, 0, tiled=True)
    both = jnp.transpose(both, (1, 0, 2, 3))
    grad_low = both[:, :, :part_rows, :].reshape(block_size, block_size)
    right_full = both[:, :, part_rows:, :].reshape(block_size, block_size)

    left_mid = jnp.dot(left_root, grad_low, preferred_element_type=jnp.float32).astype(jnp.bfloat16)
    precond = jnp.dot(left_mid, right_full, preferred_element_type=jnp.float32)
    precond_part = jnp.broadcast_to(jnp.sum(precond * precond), (owners, 1, 128))
    precond_sum = jnp.sum(lax.all_to_all(precond_part, OWN, 0, 0, tiled=True)[:, 0, 0])
    graft_scale = jnp.sqrt(adam_sum) / (jnp.sqrt(precond_sum) + norm_eps)
    master_out = master - learn_rate * graft_scale * precond
    weight_part = lax.dynamic_slice_in_dim(master_out.astype(jnp.bfloat16), core * part_rows, part_rows, 0)
    weight_rows = jnp.broadcast_to(weight_part[None], (owners, part_rows, block_size))
    weights = join_cores(lax.all_to_all(weight_rows, OWN, 0, 0, tiled=True), cores)

    my_slots = owner_index * capacity + jnp.arange(capacity, dtype=jnp.int32)
    matches = (tile_slot[:, None] == my_slots[None, :]).astype(jnp.int32)
    tile_ids = jnp.sum(matches * jnp.arange(tile_count, dtype=jnp.int32)[:, None], axis=0)
    filled = jnp.sum(matches, axis=0)
    per_half = block_size // tile_rows
    which_half = tile_ids // per_half
    offsets = (tile_ids - which_half * per_half) * tile_rows
    grad_low_t = grad_low.T
    row_blocks = jnp.concatenate(
        [lax.dynamic_slice_in_dim(grad_low, offsets[s], tile_rows, 0) for s in range(capacity)], axis=0
    )
    col_blocks = jnp.concatenate(
        [lax.dynamic_slice_in_dim(grad_low_t, offsets[s], tile_rows, 0) for s in range(capacity)], axis=0
    )
    left_tiles = lax.dot_general(
        row_blocks, grad_low, (((1,), (1,)), ((), ())), preferred_element_type=jnp.float32
    ).reshape(capacity, tile_rows, block_size)
    right_tiles = jnp.dot(col_blocks, grad_low, preferred_element_type=jnp.float32).reshape(
        capacity, tile_rows, block_size
    )
    product = jnp.where((which_half == 0)[:, None, None], left_tiles, right_tiles)
    fresh = stat_decay * stats_in + (1.0 - stat_decay) / block_size * product
    stats_out = jnp.where((filled > 0)[:, None, None], fresh, 0.0)
    return (master_out, moment_out, stats_out, weights)


def solution(mesh):
    sub_mesh = Mesh(mesh.devices.reshape(SUB_SIZES), GRP + OWN)
    rows_all = P(GRP + OWN, None)
    rows_own = P(OWN, None)
    in_specs = (rows_all, rows_all, rows_own, rows_own, rows_own, rows_own, P(OWN, None, None), P())
    out_specs = (rows_own, rows_own, P(OWN, None, None), P())
    return jax.shard_map(local, mesh=sub_mesh, in_specs=in_specs, out_specs=out_specs, check_vma=False)
```

profile of v0, /device:TPU:1, one launch (start us, length us, event | category | flops | bytes accessed | tf_op | source)
XLA Modules:
  0.0 285.1 jit_solution(16256668773336357469)
XLA Ops:
  0.6 0.0 copy-start
  0.6 0.9 copy-done
  1.6 1.7 fusion.17
  3.3 0.6 copy.34
  3.8 14.6 %all_to_all.40 = f32[2,64,8,1024]{3,2,1,0:T(8,128)} all-to-all(f32[2,64,8,1024]{3,2,1,0:T(8,128)S(1)} %bitcast.51), channel_id=1, replica_groups=mesh['yl'=4,'c'=2,'x'=4,'yh'=2,'z'=8] {'c'}, dimensions={0} | all-to-all | bytes 8388608 | tf_op jit(solution)/shard_map/all_to_all | solution.py:58
  18.5 2.8 reduce_sum.81
  21.3 61.4 %all_to_all.41 = f32[64,8,1024]{2,1,0:T(8,128)} all-to-all(f32[64,8,1024]{2,1,0:T(8,128)S(1)} %reduce_sum.81), channel_id=1, replica_groups=mesh['yl'=4,'c'=2,'x'=4,'yh'=2,'z'=8] {'x','yh','z'}, dimensions={0} | all-to-all | bytes 4194304 | tf_op jit(solution)/shard_map/all_to_all | solution.py:59
  82.7 1.8 reduce_sum.82
  84.5 0.7 broadcast_in_dim.25
  85.2 13.0 %all-to-all-start.2 = ((f32[8,8,1024]{2,1,0:T(8,128)}), f32[8,8,1024]{2,1,0:T(8,128)S(1)}, u32[]{:S(2)}, u32[]{:S(2)}) async-start(f32[8,8,1024]{2,1,0:T(8,128)} %broadcast_in_dim.25), calls=%async_computation.2 | async-start | bytes 524288 | tf_op jit(solution)/shard_map/all_to_all | solution.py:62
  98.2 0.6 compare_reduce_fusion
  98.8 8.0 %all-to-all-done.2 = f32[8,8,1024]{2,1,0:T(8,128)S(1)} async-done(((f32[8,8,1024]{2,1,0:T(8,128)}), f32[8,8,1024]{2,1,0:T(8,128)S(1)}, u32[]{:S(2)}, u32[]{:S(2)}) %all-to-all-start.2) | async-done | bytes 262176 | tf_op jit(solution)/shard_map/all_to_all | solution.py:62
  106.9 1.3 multiply_reduce_fusion.1
  112.4 2.7 fusion.12
  115.1 2.1 broadcast_in_dim.26
  117.1 4.8 %all-to-all-start.3 = ((bf16[64,17,1024]{2,1,0:T(8,128)(2,1)}), bf16[64,17,1024]{2,1,0:T(8,128)(2,1)S(1)}, u32[]{:S(2)}, u32[]{:S(2)}) async-start(bf16[64,17,1024]{2,1,0:T(8,128)(2,1)} %broadcast_in_dim.26), calls=%async_computation.3 | async-start | bytes 6291456 | tf_op jit(solution)/shard_map/all_to_all | solution.py:79
  122.0 76.2 %all-to-all-done.3 = bf16[64,17,1024]{2,1,0:T(8,128)(2,1)S(1)} async-done(((bf16[64,17,1024]{2,1,0:T(8,128)(2,1)}), bf16[64,17,1024]{2,1,0:T(8,128)(2,1)S(1)}, u32[]{:S(2)}, u32[]{:S(2)}) %all-to-all-start.3) | async-done | bytes 2228256 | tf_op jit(solution)/shard_map/all_to_all | solution.py:79
  198.2 0.5 fusion.15
  198.7 1.1 copy-done.1
  199.9 0.2 pad_maximum_fusion
  200.1 0.6 broadcast_in_dim.27
  200.7 9.3 %all_to_all.42 = bf16[2,64,16,1024]{3,2,1,0:T(8,128)(2,1)S(1)} all-to-all(bf16[2,64,16,1024]{3,2,1,0:T(8,128)(2,1)S(1)} %broadcast_in_dim.27), channel_id=1, replica_groups=mesh['yl'=4,'c'=2,'x'=4,'yh'=2,'z'=8] {'c'}, dimensions={0} | all-to-all | bytes 8388608 | tf_op jit(solution)/shard_map/all_to_all | solution.py:82
  210.0 0.8 copy.33
  210.8 0.0 copy-start.6
  210.8 1.8 fusion.14
  212.6 2.9 %multiply_reduce_fusion = (f32[]{:T(128)}, f32[16,1024]{1,0:T(8,128)S(1)}) fusion(bf16[1024,1024]{1,0:T(8,128)(2,1)} %bitcast.53, bf16[16,1024]{1,0:T(8,128)(2,1)S(1)} %copy-done.6, bf16[1024,1024]{1,0:T(8,128)(2,1)S(1)} %bitcast.45), kind=kOutput, calls=%fused_computation.22 | convolution fusion | flops 67158016 | bytes 4292612 | tf_op jit(solution)/shard_map/dot_general | solution.py:88
  215.5 1.3 broadcast_in_dim.28
  216.8 9.0 %all-to-all-start.5 = ((f32[64,1,128]{2,1,0:T(1,128)}), f32[64,1,128]{2,1,0:T(1,128)S(1)}, u32[]{:S(2)}, u32[]{:S(2)}) async-start(f32[64,1,128]{2,1,0:T(1,128)} %broadcast_in_dim.28), calls=%async_computation.5 | async-start | bytes 65536 | tf_op jit(solution)/shard_map/all_to_all | solution.py:90
  225.8 1.6 fusion.9
  228.1 10.8 %all-to-all-done.5 = f32[64,1,128]{2,1,0:T(1,128)S(1)} async-done(((f32[64,1,128]{2,1,0:T(1,128)}), f32[64,1,128]{2,1,0:T(1,128)S(1)}, u32[]{:S(2)}, u32[]{:S(2)}) %all-to-all-start.5) | async-done | bytes 32800 | tf_op jit(solution)/shard_map/all_to_all | solution.py:90
  238.9 0.7 slice_reduce_fusion
  240.4 0.6 copy-done.3
  241.0 1.1 broadcast_in_dim.35
  242.1 4.7 %all-to-all-start.6 = ((bf16[64,8,1024]{2,1,0:T(8,128)(2,1)}), bf16[64,8,1024]{2,1,0:T(8,128)(2,1)S(1)}, u32[]{:S(2)}, u32[]{:S(2)}) async-start(bf16[64,8,1024]{2,1,0:T(8,128)(2,1)} %broadcast_in_dim.35), calls=%async_computation.6 | async-start | bytes 2097152 | tf_op jit(solution)/shard_map/all_to_all | solution.py:95
  246.8 0.2 fusion.10
  247.0 0.7 fusion.16
  255.3 0.5 dynamic-slice_bitcast_fusion.3
  255.7 1.1 pad_maximum_fusion.1
  256.8 1.1 copy.28
  257.9 0.0 copy-start.2
  257.9 0.1 constant_dynamic-slice_fusion.3
  258.0 0.8 fusion.18
  258.7 0.1 copy-done.2
  258.8 1.2 fusion.2
  260.0 16.5 %all-to-all-done.6 = bf16[64,8,1024]{2,1,0:T(8,128)(2,1)S(1)} async-done(((bf16[64,8,1024]{2,1,0:T(8,128)(2,1)}), bf16[64,8,1024]{2,1,0:T(8,128)(2,1)S(1)}, u32[]{:S(2)}, u32[]{:S(2)}) %all-to-all-start.6) | async-done | bytes 1048608 | tf_op jit(solution)/shard_map/all_to_all | solution.py:95
  276.6 0.2 broadcast_in_dim.36
  276.8 6.8 %all_to_all.43 = bf16[2,64,8,1024]{3,2,1,0:T(8,128)(2,1)S(1)} all-to-all(bf16[2,64,8,1024]{3,2,1,0:T(8,128)(2,1)S(1)} %broadcast_in_dim.36), channel_id=1, replica_groups=mesh['yl'=4,'c'=2,'x'=4,'yh'=2,'z'=8] {'c'}, dimensions={0} | all-to-all | bytes 4194304 | tf_op jit(solution)/shard_map/all_to_all | solution.py:37
  283.7 1.5 copy.29
  (21 shorter events, 0.1 us)
Async XLA Ops:
  0.6 1.0 copy-start
  82.7 24.2 %copy-start.4 = (f32[16,1024]{1,0:T(8,128)S(1)}, f32[16,1024]{1,0:T(8,128)}, u32[]{:S(2)}) copy-start(f32[16,1024]{1,0:T(8,128)} %param.13) | copy-start | bytes 196612
  82.7 29.6 %copy-start.7 = (bf16[16,1024]{1,0:T(8,128)(2,1)S(1)}, bf16[16,1024]{1,0:T(8,128)(2,1)}, u32[]{:S(2)}) copy-start(bf16[16,1024]{1,0:T(8,128)(2,1)} %param.15) | copy-start | bytes 98308
  85.2 21.7 %all-to-all-start.2 = ((f32[8,8,1024]{2,1,0:T(8,128)}), f32[8,8,1024]{2,1,0:T(8,128)S(1)}, u32[]{:S(2)}, u32[]{:S(2)}) async-start(f32[8,8,1024]{2,1,0:T(8,128)} %broadcast_in_dim.25), calls=%async_computation.2 | async-start | bytes 524288 | tf_op jit(solution)/shard_map/all_to_all | solution.py:62
  117.1 81.0 %all-to-all-start.3 = ((bf16[64,17,1024]{2,1,0:T(8,128)(2,1)}), bf16[64,17,1024]{2,1,0:T(8,128)(2,1)S(1)}, u32[]{:S(2)}, u32[]{:S(2)}) async-start(bf16[64,17,1024]{2,1,0:T(8,128)(2,1)} %broadcast_in_dim.26), calls=%async_computation.3 | async-start | bytes 6291456 | tf_op jit(solution)/shard_map/all_to_all | solution.py:79
  198.2 1.7 copy-start.1
  210.8 1.8 copy-start.6
  212.6 27.7 %copy-start.5 = (f32[16,1024]{1,0:T(8,128)S(1)}, f32[16,1024]{1,0:T(8,128)}, u32[]{:S(2)}) copy-start(f32[16,1024]{1,0:T(8,128)} %param.12) | copy-start | bytes 196612
  215.5 31.3 %copy-start.8 = (s32[128]{0:T(128)S(1)}, s32[128]{0:T(128)}, u32[]{:S(2)}) copy-start(s32[128]{0:T(128)} %param.17) | copy-start | bytes 1540
  216.8 22.1 %all-to-all-start.5 = ((f32[64,1,128]{2,1,0:T(1,128)}), f32[64,1,128]{2,1,0:T(1,128)S(1)}, u32[]{:S(2)}, u32[]{:S(2)}) async-start(f32[64,1,128]{2,1,0:T(1,128)} %broadcast_in_dim.28), calls=%async_computation.5 | async-start | bytes 65536 | tf_op jit(solution)/shard_map/all_to_all | solution.py:90
  240.4 0.6 copy-start.3
  242.1 34.5 %all-to-all-start.6 = ((bf16[64,8,1024]{2,1,0:T(8,128)(2,1)}), bf16[64,8,1024]{2,1,0:T(8,128)(2,1)S(1)}, u32[]{:S(2)}, u32[]{:S(2)}) async-start(bf16[64,8,1024]{2,1,0:T(8,128)(2,1)} %broadcast_in_dim.35), calls=%async_computation.6 | async-start | bytes 2097152 | tf_op jit(solution)/shard_map/all_to_all | solution.py:95
  257.9 1.0 copy-start.2
where the time goes:
time: 286 us; the launch traced here: 285 us
  waiting for transfers between devices  112 us (39%)
  blocking collectives  92.2 us (32%)
  starting transfers between devices  31.5 us (11%)
  local copies, waits for them, and re-layouts  16.3 us (6%)
  between operations  14.1 us (5%)
  other arithmetic  13 us (5%)
  matrix products  6.56 us (2%)
    all_to_all x1, waiting for transfers between devices, local(): got = lax.all_to_all(sent, OWN, 0, 0, tiled=True)  76.2 us
    all_to_all x1, blocking collectives, local(): pieces = lax.all_to_all(chip_sum, OWN, 0, 0, tiled=True)  61.4 us
    all_to_all x1, waiting for transfers between devices, local(): lax.all_to_all(weight_rows, OWN, 0, 0, tiled=True)  16.5 us
    all_to_all x1, blocking collectives, local(): chip_sum = jnp.sum(lax.all_to_all(halves, 'c', 0, 0, tiled=True), axis=0)  14.6 us
    all_to_all x1, starting transfers between devices, local(): lax.all_to_all(copies, GRP, 0, 0, tiled=True)  13 us
    all_to_all x1, waiting for transfers between devices, local(): lax.all_to_all(precond_part, OWN, 0, 0, tiled=True)[:, 0, 0]  10.8 us
    all_to_all x1, blocking collectives, local(): lax.all_to_all(jnp.broadcast_to(mine[None], (cores,) + mine.shape), 'c',...  9.3 us
    all_to_all x1, starting transfers between devices, local(): lax.all_to_all(precond_part, OWN, 0, 0, tiled=True)[:, 0, 0]  9.02 us
  transfers between devices with their start and end apart: 4, of which 4 were waited for; matrix products, arithmetic and copies ran while one was open for 3% of the time, Pallas kernels for 0%

commit v1 on v0

--- a/solution.py
+++ b/solution.py
@@ -13,14 +13,6 @@
 GRP = ("yl", "c")
 OWN = ("x", "yh", "z")
 SUB_SIZES = (4, 2, 4, 2, 8)
-
-
-def split3(value):
-    hi = lax.reduce_precision(value, exponent_bits=8, mantissa_bits=7)
-    rest = value - hi
-    mid = lax.reduce_precision(rest, exponent_bits=8, mantissa_bits=7)
-    lo = lax.reduce_precision(rest - mid, exponent_bits=8, mantissa_bits=7)
-    return jnp.stack([hi, mid, lo])
 
 
 def gather_own_rows(block):
@@ -66,19 +58,13 @@
 
     moment_out = moment_decay * moment + (1.0 - moment_decay) * grad_rows * grad_rows
     adam_dir = grad_rows / (jnp.sqrt(moment_out) + adam_eps)
-    adam_part = split3(jnp.sum(adam_dir * adam_dir))
-
-    extra = jnp.zeros((1, block_size), jnp.float32).at[0, :3].set(adam_part)
+    adam_part = jnp.sum(adam_dir * adam_dir)
     core = lax.axis_index("c")
     my_part = lax.dynamic_slice_in_dim(grad_rows, core * part_rows, part_rows, 0)
     root_part = lax.dynamic_slice_in_dim(right_root, core * part_rows, part_rows, 0)
-    payload = jnp.concatenate(
-        [my_part.astype(jnp.bfloat16), extra.astype(jnp.bfloat16), root_part], axis=0
-    )
+    payload = jnp.concatenate([my_part.astype(jnp.bfloat16), root_part], axis=0)
     sent = jnp.broadcast_to(payload[None], (owners,) + payload.shape)
-    got = lax.all_to_all(sent, OWN, 0, 0, tiled=True)
-    adam_sum = jnp.sum(got[:, part_rows, :3].astype(jnp.float32))
-    mine = jnp.concatenate([got[:, :part_rows, :], got[:, part_rows + 1 :, :]], axis=1)
+    mine = lax.all_to_all(sent, OWN, 0, 0, tiled=True)
     both = lax.all_to_all(jnp.broadcast_to(mine[None], (cores,) + mine.shape), "c", 0, 0, tiled=True)
     both = jnp.transpose(both, (1, 0, 2, 3))
     grad_low = both[:, :, :part_rows, :].reshape(block_size, block_size)
@@ -86,8 +72,10 @@
 
     left_mid = jnp.dot(left_root, grad_low, preferred_element_type=jnp.float32).astype(jnp.bfloat16)
     precond = jnp.dot(left_mid, right_full, preferred_element_type=jnp.float32)
-    precond_part = jnp.broadcast_to(jnp.sum(precond * precond), (owners, 1, 128))
-    precond_sum = jnp.sum(lax.all_to_all(precond_part, OWN, 0, 0, tiled=True)[:, 0, 0])
+    sums = jnp.zeros((1, 128), jnp.float32).at[0, 0].set(jnp.sum(precond * precond)).at[0, 1].set(adam_part)
+    got_sums = lax.all_to_all(jnp.broadcast_to(sums[None], (owners, 1, 128)), OWN, 0, 0, tiled=True)
+    precond_sum = jnp.sum(got_sums[:, 0, 0])
+    adam_sum = jnp.sum(got_sums[:, 0, 1])
     graft_scale = jnp.sqrt(adam_sum) / (jnp.sqrt(precond_sum) + norm_eps)
     master_out = master - learn_rate * graft_scale * precond
     weight_part = lax.dynamic_slice_in_dim(master_out.astype(jnp.bfloat16), core * part_rows, part_rows, 0)

time: 286 us -> 258 us (0.902)
  waiting for transfers between devices: 112 us -> 88.8 us
  between operations: 14.1 us -> 11.2 us
    all_to_all x2, waiting for transfers between devices: 87 us -> 63.5 us  [the longest x1 50.4 us: local(): mine = lax.all_to_all(sent, OWN, 0, 0, tiled=True)]
where the time goes in v1:
time: 258 us; the launch traced here: 256 us
  blocking collectives  92.3 us (36%)
  waiting for transfers between devices  88.8 us (34%)
  starting transfers between devices  30.6 us (12%)
  local copies, waits for them, and re-layouts  15.4 us (6%)
  other arithmetic  11.6 us (4%)
  between operations  11.2 us (4%)
  matrix products  6.56 us (3%)
    all_to_all x1, blocking collectives, local(): pieces = lax.all_to_all(chip_sum, OWN, 0, 0, tiled=True)  61.4 us
    all_to_all x1, waiting for transfers between devices, local(): mine = lax.all_to_all(sent, OWN, 0, 0, tiled=True)  50.4 us
    all_to_all x1, waiting for transfers between devices, local(): lax.all_to_all(weight_rows, OWN, 0, 0, tiled=True)  16.6 us
    all_to_all x1, blocking collectives, local(): chip_sum = jnp.sum(lax.all_to_all(halves, 'c', 0, 0, tiled=True), axis=0)  14.6 us
    all_to_all x1, waiting for transfers between devices, local(): lax.all_to_all(jnp.broadcast_to(sums[None], (owners, 1, 128)), OWN, 0, 0,...  13.1 us
    all_to_all x1, starting transfers between devices, local(): lax.all_to_all(copies, GRP, 0, 0, tiled=True)  13 us
    all_to_all x1, blocking collectives, local(): lax.all_to_all(jnp.broadcast_to(mine[None], (cores,) + mine.shape), 'c',...  8.78 us
    all_to_all x1, waiting for transfers between devices, local(): lax.all_to_all(copies, GRP, 0, 0, tiled=True)  8.67 us
  transfers between devices with their start and end apart: 4, of which 4 were waited for; matrix products, arithmetic and copies ran while one was open for 3% of the time, Pallas kernels for 0%

profile of v1, /device:TPU:1, one launch (start us, length us, event | category | flops | bytes accessed | tf_op | source)
XLA Modules:
  0.0 256.4 jit_solution(6924421100772235090)
XLA Ops:
  0.6 0.0 copy-start
  0.6 0.9 copy-done
  1.6 1.7 fusion.11
  3.3 0.6 copy.36
  3.8 14.6 %all_to_all.40 = f32[2,64,8,1024]{3,2,1,0:T(8,128)} all-to-all(f32[2,64,8,1024]{3,2,1,0:T(8,128)S(1)} %bitcast.56), channel_id=1, replica_groups=mesh['yl'=4,'c'=2,'x'=4,'yh'=2,'z'=8] {'c'}, dimensions={0} | all-to-all | bytes 8388608 | tf_op jit(solution)/shard_map/all_to_all | solution.py:50
  18.5 2.8 %reduce_sum.81 = f32[64,8,1024]{2,1,0:T(8,128)S(1)} reduce(f32[2,64,8,1024]{3,2,1,0:T(8,128)} %all_to_all.40, f32[]{:T(128)} %constant.98.clone.1), dimensions={0}, to_apply=%region_1.0 | reduce | flops 524288 | bytes 6291460 | tf_op jit(solution)/shard_map/reduce_sum | solution.py:50
  21.3 61.4 %all_to_all.41 = f32[64,8,1024]{2,1,0:T(8,128)} all-to-all(f32[64,8,1024]{2,1,0:T(8,128)S(1)} %reduce_sum.81), channel_id=1, replica_groups=mesh['yl'=4,'c'=2,'x'=4,'yh'=2,'z'=8] {'x','yh','z'}, dimensions={0} | all-to-all | bytes 4194304 | tf_op jit(solution)/shard_map/all_to_all | solution.py:51
  82.7 1.7 reduce_sum.82
  84.5 0.7 broadcast_in_dim.29
  85.2 13.0 %all-to-all-start.2 = ((f32[8,8,1024]{2,1,0:T(8,128)}), f32[8,8,1024]{2,1,0:T(8,128)S(1)}, u32[]{:S(2)}, u32[]{:S(2)}) async-start(f32[8,8,1024]{2,1,0:T(8,128)} %broadcast_in_dim.29), calls=%async_computation.2 | async-start | bytes 524288 | tf_op jit(solution)/shard_map/all_to_all | solution.py:54
  98.2 8.7 %all-to-all-done.2 = f32[8,8,1024]{2,1,0:T(8,128)S(1)} async-done(((f32[8,8,1024]{2,1,0:T(8,128)}), f32[8,8,1024]{2,1,0:T(8,128)S(1)}, u32[]{:S(2)}, u32[]{:S(2)}) %all-to-all-start.2) | async-done | bytes 262176 | tf_op jit(solution)/shard_map/all_to_all | solution.py:54
  106.9 1.6 broadcast_in_dim.30
  108.5 5.0 %all-to-all-start.3 = ((bf16[64,16,1024]{2,1,0:T(8,128)(2,1)}), bf16[64,16,1024]{2,1,0:T(8,128)(2,1)S(1)}, u32[]{:S(2)}, u32[]{:S(2)}) async-start(bf16[64,16,1024]{2,1,0:T(8,128)(2,1)} %broadcast_in_dim.30), calls=%async_computation.3 | async-start | bytes 4194304 | tf_op jit(solution)/shard_map/all_to_all | solution.py:67
  113.5 0.7 slice.65
  114.1 0.6 compare_reduce_fusion.1
  114.8 0.6 compare_reduce_fusion
  115.4 1.3 multiply_reduce_fusion
  116.7 50.4 %all-to-all-done.3 = bf16[64,16,1024]{2,1,0:T(8,128)(2,1)S(1)} async-done(((bf16[64,16,1024]{2,1,0:T(8,128)(2,1)}), bf16[64,16,1024]{2,1,0:T(8,128)(2,1)S(1)}, u32[]{:S(2)}, u32[]{:S(2)}) %all-to-all-start.3) | async-done | bytes 2097184 | tf_op jit(solution)/shard_map/all_to_all | solution.py:67
  167.1 0.5 broadcast_in_dim.31
  167.6 8.8 %all_to_all.42 = bf16[2,64,16,1024]{3,2,1,0:T(8,128)(2,1)S(1)} all-to-all(bf16[2,64,16,1024]{3,2,1,0:T(8,128)(2,1)S(1)} %broadcast_in_dim.31), channel_id=1, replica_groups=mesh['yl'=4,'c'=2,'x'=4,'yh'=2,'z'=8] {'c'}, dimensions={0} | all-to-all | bytes 8388608 | tf_op jit(solution)/shard_map/all_to_all | solution.py:68
  176.4 0.8 copy.35
  177.2 0.0 copy-start.5
  177.2 1.8 fusion.8
  179.0 2.9 %multiply_reduce_fusion.1 = (f32[]{:T(128)}, f32[16,1024]{1,0:T(8,128)S(1)}) fusion(bf16[1024,1024]{1,0:T(8,128)(2,1)} %bitcast.58, bf16[16,1024]{1,0:T(8,128)(2,1)S(1)} %copy-done.5, bf16[1024,1024]{1,0:T(8,128)(2,1)S(1)} %bitcast.50), kind=kOutput, calls=%fused_computation.18 | convolution fusion | flops 67158016 | bytes 4292612 | tf_op jit(solution)/shard_map/dot_general | solution.py:74
  183.2 2.5 fusion.10
  185.7 1.4 bitcast_dynamic-update-slice_fusion
  187.1 0.6 broadcast_in_dim.37
  187.7 8.0 %all-to-all-start.5 = ((f32[64,1,128]{2,1,0:T(1,128)}), f32[64,1,128]{2,1,0:T(1,128)S(1)}, u32[]{:S(2)}, u32[]{:S(2)}) async-start(f32[64,1,128]{2,1,0:T(1,128)} %broadcast_in_dim.37), calls=%async_computation.5 | async-start | bytes 65536 | tf_op jit(solution)/shard_map/all_to_all | solution.py:76
  195.7 13.1 %all-to-all-done.5 = f32[64,1,128]{2,1,0:T(1,128)S(1)} async-done(((f32[64,1,128]{2,1,0:T(1,128)}), f32[64,1,128]{2,1,0:T(1,128)S(1)}, u32[]{:S(2)}, u32[]{:S(2)}) %all-to-all-start.5) | async-done | bytes 32800 | tf_op jit(solution)/shard_map/all_to_all | solution.py:76
  208.8 0.7 slice_reduce_fusion
  211.0 0.0 copy-start.2
  211.0 0.6 copy-done.2
  211.6 1.1 broadcast_in_dim.75
  212.7 4.7 %all-to-all-start.6 = ((bf16[64,8,1024]{2,1,0:T(8,128)(2,1)}), bf16[64,8,1024]{2,1,0:T(8,128)(2,1)S(1)}, u32[]{:S(2)}, u32[]{:S(2)}) async-start(bf16[64,8,1024]{2,1,0:T(8,128)(2,1)} %broadcast_in_dim.75), calls=%async_computation.6 | async-start | bytes 2097152 | tf_op jit(solution)/shard_map/all_to_all | solution.py:83
  217.4 0.2 fusion.5
  217.6 0.7 fusion.9
  225.9 0.4 dynamic-slice_bitcast_fusion.3
  226.3 1.1 pad_maximum_fusion
  227.4 1.1 copy.29
  228.5 0.0 copy-start.1
  228.5 0.1 constant_dynamic-slice_fusion.3
  228.6 0.8 fusion.12
  229.3 0.1 copy-done.1
  229.4 1.2 fusion.2
  230.6 16.6 %all-to-all-done.6 = bf16[64,8,1024]{2,1,0:T(8,128)(2,1)S(1)} async-done(((bf16[64,8,1024]{2,1,0:T(8,128)(2,1)}), bf16[64,8,1024]{2,1,0:T(8,128)(2,1)S(1)}, u32[]{:S(2)}, u32[]{:S(2)}) %all-to-all-start.6) | async-done | bytes 1048608 | tf_op jit(solution)/shard_map/all_to_all | solution.py:83
  247.3 0.2 broadcast_in_dim.76
  247.5 7.4 %all_to_all.43 = bf16[2,64,8,1024]{3,2,1,0:T(8,128)(2,1)S(1)} all-to-all(bf16[2,64,8,1024]{3,2,1,0:T(8,128)(2,1)S(1)} %broadcast_in_dim.76), channel_id=1, replica_groups=mesh['yl'=4,'c'=2,'x'=4,'yh'=2,'z'=8] {'c'}, dimensions={0} | all-to-all | bytes 4194304 | tf_op jit(solution)/shard_map/all_to_all | solution.py:29
  254.9 1.5 copy.30
  (21 shorter events, 0.1 us)
Async XLA Ops:
  0.6 1.0 copy-start
  82.7 24.1 %copy-start.6 = (bf16[16,1024]{1,0:T(8,128)(2,1)S(1)}, bf16[16,1024]{1,0:T(8,128)(2,1)}, u32[]{:S(2)}) copy-start(bf16[16,1024]{1,0:T(8,128)(2,1)} %param.17) | copy-start | bytes 98308
  85.2 21.7 %all-to-all-start.2 = ((f32[8,8,1024]{2,1,0:T(8,128)}), f32[8,8,1024]{2,1,0:T(8,128)S(1)}, u32[]{:S(2)}, u32[]{:S(2)}) async-start(f32[8,8,1024]{2,1,0:T(8,128)} %broadcast_in_dim.29), calls=%async_computation.2 | async-start | bytes 524288 | tf_op jit(solution)/shard_map/all_to_all | solution.py:54
  108.5 6.9 %copy-start.3 = (f32[16,1024]{1,0:T(8,128)S(1)}, f32[16,1024]{1,0:T(8,128)}, u32[]{:S(2)}) copy-start(f32[16,1024]{1,0:T(8,128)} %param.15) | copy-start | bytes 196612
  108.5 58.6 %all-to-all-start.3 = ((bf16[64,16,1024]{2,1,0:T(8,128)(2,1)}), bf16[64,16,1024]{2,1,0:T(8,128)(2,1)S(1)}, u32[]{:S(2)}, u32[]{:S(2)}) async-start(bf16[64,16,1024]{2,1,0:T(8,128)(2,1)} %broadcast_in_dim.30), calls=%async_computation.3 | async-start | bytes 4194304 | tf_op jit(solution)/shard_map/all_to_all | solution.py:67
  177.2 1.8 copy-start.5
  179.0 32.0 %copy-start.4 = (f32[16,1024]{1,0:T(8,128)S(1)}, f32[16,1024]{1,0:T(8,128)}, u32[]{:S(2)}) copy-start(f32[16,1024]{1,0:T(8,128)} %param.14) | copy-start | bytes 196612
  181.9 35.5 %copy-start.7 = (s32[128]{0:T(128)S(1)}, s32[128]{0:T(128)}, u32[]{:S(2)}) copy-start(s32[128]{0:T(128)} %param.19) | copy-start | bytes 1540
  187.7 21.1 %all-to-all-start.5 = ((f32[64,1,128]{2,1,0:T(1,128)}), f32[64,1,128]{2,1,0:T(1,128)S(1)}, u32[]{:S(2)}, u32[]{:S(2)}) async-start(f32[64,1,128]{2,1,0:T(1,128)} %broadcast_in_dim.37), calls=%async_computation.5 | async-start | bytes 65536 | tf_op jit(solution)/shard_map/all_to_all | solution.py:76
  211.0 0.6 copy-start.2
  212.7 34.5 %all-to-all-start.6 = ((bf16[64,8,1024]{2,1,0:T(8,128)(2,1)}), bf16[64,8,1024]{2,1,0:T(8,128)(2,1)S(1)}, u32[]{:S(2)}, u32[]{:S(2)}) async-start(bf16[64,8,1024]{2,1,0:T(8,128)(2,1)} %broadcast_in_dim.75), calls=%async_computation.6 | async-start | bytes 2097152 | tf_op jit(solution)/shard_map/all_to_all | solution.py:83
  228.5 1.0 copy-start.1

commit v2 on v1

--- a/solution.py
+++ b/solution.py
@@ -45,16 +45,18 @@
         activations, out_grads, (((0,), (0,)), ((), ())), preferred_element_type=jnp.float32
     )
     cores = SUB_SIZES[1]
+    lows = SUB_SIZES[0]
     part_rows = owner_rows // cores
-    halves = jnp.transpose(partial.reshape(owners, cores, part_rows, block_size), (1, 0, 2, 3))
+    bit_rows = part_rows // lows
+    split = partial.reshape(owners, cores, lows, bit_rows, block_size)
+    halves = jnp.transpose(split, (1, 0, 2, 3, 4))
     chip_sum = jnp.sum(lax.all_to_all(halves, "c", 0, 0, tiled=True), axis=0)
-    pieces = lax.all_to_all(chip_sum, OWN, 0, 0, tiled=True)
-    own_sum = jnp.sum(pieces, axis=0)
-    copies = jnp.broadcast_to(own_sum[None], (grp_size, part_rows, block_size))
-    got_grp = lax.all_to_all(copies, GRP, 0, 0, tiled=True).reshape(
-        SUB_SIZES[0], cores, part_rows, block_size
-    )
-    grad_rows = jnp.sum(got_grp, axis=0).reshape(owner_rows, block_size)
+    quarters = jnp.transpose(chip_sum, (1, 0, 2, 3))
+    low_sum = jnp.sum(lax.all_to_all(quarters, "yl", 0, 0, tiled=True), axis=0)
+    own_sum = jnp.sum(lax.all_to_all(low_sum, OWN, 0, 0, tiled=True), axis=0)
+    copies = jnp.broadcast_to(own_sum[None], (grp_size, bit_rows, block_size))
+    got_grp = lax.all_to_all(copies, GRP, 0, 0, tiled=True).reshape(lows, cores, bit_rows, block_size)
+    grad_rows = jnp.transpose(got_grp, (1, 0, 2, 3)).reshape(owner_rows, block_size)
 
     moment_out = moment_decay * moment + (1.0 - moment_decay) * grad_rows * grad_rows
     adam_dir = grad_rows / (jnp.sqrt(moment_out) + adam_eps)

time: 258 us -> 285 us (1.10); the launches traced: 256 us -> 280 us
  blocking collectives: 92.3 us -> 118 us
  waiting for transfers between devices: 88.8 us -> 74.5 us
  local copies, waits for them, and re-layouts: 15.4 us -> 25.3 us
  other arithmetic: 11.6 us -> 14.5 us
    all_to_all x1 -> x2, blocking collectives: 61.4 us -> 82.4 us  [the longest x1 50.4 us: local(): low_sum = jnp.sum(lax.all_to_all(quarters, 'yl', 0, 0, tiled=True), axis=0)]
    reshape x1 -> x3, local copies, waits for them, and re-layouts: 0.58 us -> 9.68 us  [the longest x2 9.63 us: local(): split = partial.reshape(owners, cores, lows, bit_rows, block_size)]
    all_to_all x1, starting transfers between devices: 13 us -> 6.66 us  [local(): lax.all_to_all(copies, GRP, 0, 0, tiled=True)]
    all_to_all x1, waiting for transfers between devices: 50.4 us -> 44.3 us  [local(): mine = lax.all_to_all(sent, OWN, 0, 0, tiled=True)]
    all_to_all x1, waiting for transfers between devices: 16.6 us -> 12.1 us  [local(): lax.all_to_all(weight_rows, OWN, 0, 0, tiled=True)]
    all_to_all x1, waiting for transfers between devices: 8.67 us -> 5.06 us  [local(): lax.all_to_all(copies, GRP, 0, 0, tiled=True)]
    reduce_sum x1, other arithmetic: 2.78 us -> 5.99 us  [local(): chip_sum = jnp.sum(lax.all_to_all(halves, 'c', 0, 0, tiled=True), axis=0)]
where the time goes in v2:
time: 285 us; the launch traced here: 280 us
  blocking collectives  118 us (41%)
  waiting for transfers between devices  74.5 us (26%)
  starting transfers between devices  28 us (10%)
  local copies, waits for them, and re-layouts  25.3 us (9%)
  other arithmetic  14.5 us (5%)
  between operations  11.2 us (4%)
  matrix products  8.49 us (3%)
    all_to_all x1, blocking collectives, local(): low_sum = jnp.sum(lax.all_to_all(quarters, 'yl', 0, 0, tiled=True), axis=0)  50.4 us
    all_to_all x1, waiting for transfers between devices, local(): mine = lax.all_to_all(sent, OWN, 0, 0, tiled=True)  44.3 us
    all_to_all x1, blocking collectives, local(): own_sum = jnp.sum(lax.all_to_all(low_sum, OWN, 0, 0, tiled=True), axis=0)  32 us
    all_to_all x1, blocking collectives, local(): chip_sum = jnp.sum(lax.all_to_all(halves, 'c', 0, 0, tiled=True), axis=0)  14.6 us
    all_to_all x1, waiting for transfers between devices, local(): lax.all_to_all(jnp.broadcast_to(sums[None], (owners, 1, 128)), OWN, 0, 0,...  13.1 us
    all_to_all x1, waiting for transfers between devices, local(): lax.all_to_all(weight_rows, OWN, 0, 0, tiled=True)  12.1 us
    all_to_all x1, blocking collectives, local(): lax.all_to_all(jnp.broadcast_to(mine[None], (cores,) + mine.shape), 'c',...  11.4 us
    all_to_all x1, starting transfers between devices, local(): lax.all_to_all(jnp.broadcast_to(sums[None], (owners, 1, 128)), OWN, 0, 0,...  10.2 us
  transfers between devices with their start and end apart: 4, of which 4 were waited for; matrix products, arithmetic and copies ran while one was open for 3% of the time, Pallas kernels for 0%

profile of v2, /device:TPU:1, one launch (start us, length us, event | category | flops | bytes accessed | tf_op | source)
XLA Modules:
  0.0 280.1 jit_solution(2425914073713119639)
XLA Ops:
  0.6 0.9 copy-done
  1.6 3.6 %fusion.11 = f32[1024,1024]{1,0:T(8,128)} fusion(bf16[128,1024]{1,0:T(8,128)(2,1)S(1)} %copy-done, bf16[128,1024]{1,0:T(8,128)(2,1)} %param.13), kind=kOutput, calls=%fused_computation.50 | convolution fusion | flops 268435456 | bytes 4718592 | tf_op jit(solution)/shard_map/dot_general | solution.py:44
  5.2 5.8 %reshape.136 = f32[64,2,4,2,1024]{4,3,2,1,0:T(2,128)} reshape(f32[1024,1024]{1,0:T(8,128)} %fusion.11) | data formatting | bytes 8388608 | tf_op jit(solution)/shard_map/reshape | solution.py:51
  11.0 3.8 %copy.52 = f32[64,2,4,2,1024]{4,3,2,0,1:T(2,128)S(1)} copy(f32[64,2,4,2,1024]{4,3,2,1,0:T(2,128)} %reshape.136) | data formatting | bytes 8388608 | tf_op jit(solution)/shard_map/reshape | solution.py:51
  14.8 14.6 %all_to_all.45 = f32[2,64,4,2,1024]{4,3,2,1,0:T(2,128)} all-to-all(f32[2,64,4,2,1024]{4,3,2,1,0:T(2,128)S(1)} %bitcast.54), channel_id=1, replica_groups=mesh['yl'=4,'c'=2,'x'=4,'yh'=2,'z'=8] {'c'}, dimensions={0} | all-to-all | bytes 8388608 | tf_op jit(solution)/shard_map/all_to_all | solution.py:53
  29.5 6.0 %reduce_sum.81 = f32[64,4,2,1024]{3,2,1,0:T(2,128)S(1)} reduce(f32[2,64,4,2,1024]{4,3,2,1,0:T(2,128)} %all_to_all.45, f32[]{:T(128)} %constant.98.clone.1), dimensions={0}, to_apply=%region_1.0 | reduce | flops 524288 | bytes 6291460 | tf_op jit(solution)/shard_map/reduce_sum | solution.py:53
  35.5 0.8 copy.38
  36.3 50.4 %all_to_all.46 = f32[4,64,2,1024]{3,2,1,0:T(2,128)S(1)} all-to-all(f32[4,64,2,1024]{3,2,1,0:T(2,128)S(1)} %copy.38), channel_id=1, replica_groups=mesh['yl'=4,'c'=2,'x'=4,'yh'=2,'z'=8] {'yl'}, dimensions={0} | all-to-all | bytes 4194304 | tf_op jit(solution)/shard_map/all_to_all | solution.py:55
  86.7 1.3 reduce_sum.82
  87.9 32.0 %all_to_all.47 = f32[64,2,1024]{2,1,0:T(2,128)S(1)} all-to-all(f32[64,2,1024]{2,1,0:T(2,128)S(1)} %reduce_sum.82), channel_id=1, replica_groups=mesh['yl'=4,'c'=2,'x'=4,'yh'=2,'z'=8] {'x','yh','z'}, dimensions={0} | all-to-all | bytes 1048576 | tf_op jit(solution)/shard_map/all_to_all | solution.py:56
  119.9 0.2 reduce_sum.83
  120.1 0.6 broadcast_in_dim.29
  120.8 6.7 %all-to-all-start.3 = ((f32[8,2,1024]{2,1,0:T(2,128)}), f32[8,2,1024]{2,1,0:T(2,128)S(1)}, u32[]{:S(2)}, u32[]{:S(2)}) async-start(f32[8,2,1024]{2,1,0:T(2,128)} %broadcast_in_dim.29), calls=%async_computation.3 | async-start | bytes 131072 | tf_op jit(solution)/shard_map/all_to_all | solution.py:58
  127.4 5.1 %all-to-all-done.3 = f32[8,2,1024]{2,1,0:T(2,128)S(1)} async-done(((f32[8,2,1024]{2,1,0:T(2,128)}), f32[8,2,1024]{2,1,0:T(2,128)S(1)}, u32[]{:S(2)}, u32[]{:S(2)}) %all-to-all-start.3) | async-done | bytes 65568 | tf_op jit(solution)/shard_map/all_to_all | solution.py:58
  132.6 1.6 broadcast_in_dim.30
  134.2 6.5 %all-to-all-start.4 = ((bf16[64,16,1024]{2,1,0:T(8,128)(2,1)}), bf16[64,16,1024]{2,1,0:T(8,128)(2,1)S(1)}, u32[]{:S(2)}, u32[]{:S(2)}) async-start(bf16[64,16,1024]{2,1,0:T(8,128)(2,1)} %broadcast_in_dim.30), calls=%async_computation.4 | async-start | bytes 4194304 | tf_op jit(solution)/shard_map/all_to_all | solution.py:69
  140.7 0.7 slice.65
  141.3 0.6 compare_reduce_fusion.1
  142.0 0.6 compare_reduce_fusion
  142.6 1.3 multiply_reduce_fusion
  143.9 44.3 %all-to-all-done.4 = bf16[64,16,1024]{2,1,0:T(8,128)(2,1)S(1)} async-done(((bf16[64,16,1024]{2,1,0:T(8,128)(2,1)}), bf16[64,16,1024]{2,1,0:T(8,128)(2,1)S(1)}, u32[]{:S(2)}, u32[]{:S(2)}) %all-to-all-start.4) | async-done | bytes 2097184 | tf_op jit(solution)/shard_map/all_to_all | solution.py:69
  188.2 0.5 broadcast_in_dim.31
  188.7 11.4 %all_to_all.48 = bf16[2,64,16,1024]{3,2,1,0:T(8,128)(2,1)S(1)} all-to-all(bf16[2,64,16,1024]{3,2,1,0:T(8,128)(2,1)S(1)} %broadcast_in_dim.31), channel_id=1, replica_groups=mesh['yl'=4,'c'=2,'x'=4,'yh'=2,'z'=8] {'c'}, dimensions={0} | all-to-all | bytes 8388608 | tf_op jit(solution)/shard_map/all_to_all | solution.py:70
  200.1 0.8 copy.51
  201.0 1.8 fusion.8
  202.7 2.9 %multiply_reduce_fusion.1 = (f32[]{:T(128)}, f32[16,1024]{1,0:T(8,128)S(1)}) fusion(bf16[1024,1024]{1,0:T(8,128)(2,1)} %bitcast.56, bf16[16,1024]{1,0:T(8,128)(2,1)S(1)} %copy-done.5, bf16[1024,1024]{1,0:T(8,128)(2,1)S(1)} %bitcast.48), kind=kOutput, calls=%fused_computation.18 | convolution fusion | flops 67158016 | bytes 4292612 | tf_op jit(solution)/shard_map/dot_general | solution.py:76
  207.0 2.5 fusion.10
  209.4 1.4 bitcast_dynamic-update-slice_fusion
  210.8 0.6 broadcast_in_dim.37
  211.4 10.2 %all-to-all-start.6 = ((f32[64,1,128]{2,1,0:T(1,128)}), f32[64,1,128]{2,1,0:T(1,128)S(1)}, u32[]{:S(2)}, u32[]{:S(2)}) async-start(f32[64,1,128]{2,1,0:T(1,128)} %broadcast_in_dim.37), calls=%async_computation.6 | async-start | bytes 65536 | tf_op jit(solution)/shard_map/all_to_all | solution.py:78
  221.7 13.1 %all-to-all-done.6 = f32[64,1,128]{2,1,0:T(1,128)S(1)} async-done(((f32[64,1,128]{2,1,0:T(1,128)}), f32[64,1,128]{2,1,0:T(1,128)S(1)}, u32[]{:S(2)}, u32[]{:S(2)}) %all-to-all-start.6) | async-done | bytes 32800 | tf_op jit(solution)/shard_map/all_to_all | solution.py:78
  234.8 0.7 slice_reduce_fusion
  237.0 0.6 copy-done.2
  237.6 1.1 broadcast_in_dim.75
  238.7 4.7 %all-to-all-start.7 = ((bf16[64,8,1024]{2,1,0:T(8,128)(2,1)}), bf16[64,8,1024]{2,1,0:T(8,128)(2,1)S(1)}, u32[]{:S(2)}, u32[]{:S(2)}) async-start(bf16[64,8,1024]{2,1,0:T(8,128)(2,1)} %broadcast_in_dim.75), calls=%async_computation.7 | async-start | bytes 2097152 | tf_op jit(solution)/shard_map/all_to_all | solution.py:85
  243.4 0.2 fusion.5
  243.6 0.7 fusion.9
  251.9 0.4 dynamic-slice_bitcast_fusion.3
  252.3 1.1 pad_maximum_fusion
  253.4 1.1 copy.44
  254.4 0.1 constant_dynamic-slice_fusion.3
  254.5 0.8 fusion.12
  255.3 0.1 copy-done.1
  255.4 1.2 fusion.2
  256.6 12.1 %all-to-all-done.7 = bf16[64,8,1024]{2,1,0:T(8,128)(2,1)S(1)} async-done(((bf16[64,8,1024]{2,1,0:T(8,128)(2,1)}), bf16[64,8,1024]{2,1,0:T(8,128)(2,1)S(1)}, u32[]{:S(2)}, u32[]{:S(2)}) %all-to-all-start.7) | async-done | bytes 1048608 | tf_op jit(solution)/shard_map/all_to_all | solution.py:85
  268.7 0.2 broadcast_in_dim.76
  268.9 9.7 %all_to_all.49 = bf16[2,64,8,1024]{3,2,1,0:T(8,128)(2,1)S(1)} all-to-all(bf16[2,64,8,1024]{3,2,1,0:T(8,128)(2,1)S(1)} %broadcast_in_dim.76), channel_id=1, replica_groups=mesh['yl'=4,'c'=2,'x'=4,'yh'=2,'z'=8] {'c'}, dimensions={0} | all-to-all | bytes 4194304 | tf_op jit(solution)/shard_map/all_to_all | solution.py:29
  278.6 1.5 copy.45
  (26 shorter events, 0.2 us)
Async XLA Ops:
  0.6 1.0 copy-start
  86.7 45.9 %copy-start.6 = (bf16[16,1024]{1,0:T(8,128)(2,1)S(1)}, bf16[16,1024]{1,0:T(8,128)(2,1)}, u32[]{:S(2)}) copy-start(bf16[16,1024]{1,0:T(8,128)(2,1)} %param.17) | copy-start | bytes 98308
  120.8 11.7 %all-to-all-start.3 = ((f32[8,2,1024]{2,1,0:T(2,128)}), f32[8,2,1024]{2,1,0:T(2,128)S(1)}, u32[]{:S(2)}, u32[]{:S(2)}) async-start(f32[8,2,1024]{2,1,0:T(2,128)} %broadcast_in_dim.29), calls=%async_computation.3 | async-start | bytes 131072 | tf_op jit(solution)/shard_map/all_to_all | solution.py:58
  134.2 8.4 %copy-start.3 = (f32[16,1024]{1,0:T(8,128)S(1)}, f32[16,1024]{1,0:T(8,128)}, u32[]{:S(2)}) copy-start(f32[16,1024]{1,0:T(8,128)} %param.15) | copy-start | bytes 196612
  134.2 54.0 %all-to-all-start.4 = ((bf16[64,16,1024]{2,1,0:T(8,128)(2,1)}), bf16[64,16,1024]{2,1,0:T(8,128)(2,1)S(1)}, u32[]{:S(2)}, u32[]{:S(2)}) async-start(bf16[64,16,1024]{2,1,0:T(8,128)(2,1)} %broadcast_in_dim.30), calls=%async_computation.4 | async-start | bytes 4194304 | tf_op jit(solution)/shard_map/all_to_all | solution.py:69
  200.9 1.8 copy-start.5
  202.7 34.2 %copy-start.4 = (f32[16,1024]{1,0:T(8,128)S(1)}, f32[16,1024]{1,0:T(8,128)}, u32[]{:S(2)}) copy-start(f32[16,1024]{1,0:T(8,128)} %param.14) | copy-start | bytes 196612
  205.6 37.7 %copy-start.7 = (s32[128]{0:T(128)S(1)}, s32[128]{0:T(128)}, u32[]{:S(2)}) copy-start(s32[128]{0:T(128)} %param.19) | copy-start | bytes 1540
  211.4 23.3 %all-to-all-start.6 = ((f32[64,1,128]{2,1,0:T(1,128)}), f32[64,1,128]{2,1,0:T(1,128)S(1)}, u32[]{:S(2)}, u32[]{:S(2)}) async-start(f32[64,1,128]{2,1,0:T(1,128)} %broadcast_in_dim.37), calls=%async_computation.6 | async-start | bytes 65536 | tf_op jit(solution)/shard_map/all_to_all | solution.py:78
  237.0 0.6 copy-start.2
  238.7 30.0 %all-to-all-start.7 = ((bf16[64,8,1024]{2,1,0:T(8,128)(2,1)}), bf16[64,8,1024]{2,1,0:T(8,128)(2,1)S(1)}, u32[]{:S(2)}, u32[]{:S(2)}) async-start(bf16[64,8,1024]{2,1,0:T(8,128)(2,1)} %broadcast_in_dim.75), calls=%async_computation.7 | async-start | bytes 2097152 | tf_op jit(solution)/shard_map/all_to_all | solution.py:85
  254.4 1.0 copy-start.1

commit v3 on v1

--- a/solution.py
+++ b/solution.py
@@ -41,6 +41,13 @@
     grp_size = SUB_SIZES[0] * SUB_SIZES[1]
 
 
+    cores_r = SUB_SIZES[1]
+    root_part = lax.dynamic_slice_in_dim(
+        right_root, lax.axis_index("c") * (owner_rows // cores_r), owner_rows // cores_r, 0
+    )
+    roots_got = lax.all_to_all(
+        jnp.broadcast_to(root_part[None], (owners,) + root_part.shape), OWN, 0, 0, tiled=True
+    )
     partial = lax.dot_general(
         activations, out_grads, (((0,), (0,)), ((), ())), preferred_element_type=jnp.float32
     )
@@ -61,10 +68,9 @@
     adam_part = jnp.sum(adam_dir * adam_dir)
     core = lax.axis_index("c")
     my_part = lax.dynamic_slice_in_dim(grad_rows, core * part_rows, part_rows, 0)
-    root_part = lax.dynamic_slice_in_dim(right_root, core * part_rows, part_rows, 0)
-    payload = jnp.concatenate([my_part.astype(jnp.bfloat16), root_part], axis=0)
+    payload = my_part.astype(jnp.bfloat16)
     sent = jnp.broadcast_to(payload[None], (owners,) + payload.shape)
-    mine = lax.all_to_all(sent, OWN, 0, 0, tiled=True)
+    mine = jnp.concatenate([lax.all_to_all(sent, OWN, 0, 0, tiled=True), roots_got], axis=1)
     both = lax.all_to_all(jnp.broadcast_to(mine[None], (cores,) + mine.shape), "c", 0, 0, tiled=True)
     both = jnp.transpose(both, (1, 0, 2, 3))
     grad_low = both[:, :, :part_rows, :].reshape(block_size, block_size)

time: 258 us -> 274 us (1.062); the launches traced: 256 us -> 269 us
  starting transfers between devices: 30.6 us -> 40.8 us
  blocking collectives: 92.3 us -> 97.9 us
  waiting for transfers between devices: 88.8 us -> 83.5 us
    all_to_all x1 -> x2, starting transfers between devices: 4.97 us -> 12.4 us  [the longest x1 7.53 us: local(): lax.all_to_all(sent, OWN, 0, 0, tiled=True)]
    all_to_all x1, waiting for transfers between devices: 16.6 us -> 10.9 us  [local(): lax.all_to_all(weight_rows, OWN, 0, 0, tiled=True)]
    all_to_all x1, blocking collectives: 8.78 us -> 12.3 us  [local(): lax.all_to_all(jnp.broadcast_to(mine[None], (cores,) + mine.shape), 'c',...]
    all_to_all x1 -> x2, waiting for transfers between devices: 50.4 us -> 50.7 us  [the longest x1 30.1 us: local(): lax.all_to_all(jnp.broadcast_to(root_part[None], (owners,) + root_part.sh...]
  transfers between devices with their start and end apart: 4 -> 5, of which waited for: 4 -> 5; matrix products, arithmetic and copies ran while one was open for 3% -> 3% of each run, Pallas kernels for 0% -> 0%
where the time goes in v3:
time: 274 us; the launch traced here: 269 us
  blocking collectives  97.9 us (36%)
  waiting for transfers between devices  83.5 us (30%)
  starting transfers between devices  40.8 us (15%)
  local copies, waits for them, and re-layouts  16 us (6%)
  other arithmetic  13.1 us (5%)
  between operations  11.2 us (4%)
  matrix products  6.56 us (2%)
    all_to_all x1, blocking collectives, local(): pieces = lax.all_to_all(chip_sum, OWN, 0, 0, tiled=True)  60.8 us
    all_to_all x1, waiting for transfers between devices, local(): lax.all_to_all(jnp.broadcast_to(root_part[None], (owners,) + root_part.sh...  30.1 us
    all_to_all x1, waiting for transfers between devices, local(): lax.all_to_all(sent, OWN, 0, 0, tiled=True)  20.6 us
    all_to_all x1, blocking collectives, local(): chip_sum = jnp.sum(lax.all_to_all(halves, 'c', 0, 0, tiled=True), axis=0)  14.6 us
    all_to_all x1, starting transfers between devices, local(): lax.all_to_all(copies, GRP, 0, 0, tiled=True)  13.6 us
    all_to_all x1, waiting for transfers between devices, local(): lax.all_to_all(jnp.broadcast_to(sums[None], (owners, 1, 128)), OWN, 0, 0,...  13.1 us
    all_to_all x1, blocking collectives, local(): lax.all_to_all(jnp.broadcast_to(mine[None], (cores,) + mine.shape), 'c',...  12.3 us
    all_to_all x1, waiting for transfers between devices, local(): lax.all_to_all(weight_rows, OWN, 0, 0, tiled=True)  10.9 us
  transfers between devices with their start and end apart: 5, of which 5 were waited for; matrix products, arithmetic and copies ran while one was open for 3% of the time, Pallas kernels for 0%

profile of v3, /device:TPU:1, one launch (start us, length us, event | category | flops | bytes accessed | tf_op | source)
XLA Modules:
  0.0 269.0 jit_solution(10086776807391940313)
XLA Ops:
  0.6 0.9 copy-done
  1.6 1.7 fusion.11
  3.3 0.6 copy.36
  3.8 14.6 %all_to_all.45 = f32[2,64,8,1024]{3,2,1,0:T(8,128)} all-to-all(f32[2,64,8,1024]{3,2,1,0:T(8,128)S(1)} %bitcast.56), channel_id=1, replica_groups=mesh['yl'=4,'c'=2,'x'=4,'yh'=2,'z'=8] {'c'}, dimensions={0} | all-to-all | bytes 8388608 | tf_op jit(solution)/shard_map/all_to_all | solution.py:57
  18.5 2.8 %reduce_sum.81 = f32[64,8,1024]{2,1,0:T(8,128)S(1)} reduce(f32[2,64,8,1024]{3,2,1,0:T(8,128)} %all_to_all.45, f32[]{:T(128)} %constant.98.clone.1), dimensions={0}, to_apply=%region_1.0 | reduce | flops 524288 | bytes 6291460 | tf_op jit(solution)/shard_map/reduce_sum | solution.py:57
  21.3 60.8 %all_to_all.46 = f32[64,8,1024]{2,1,0:T(8,128)} all-to-all(f32[64,8,1024]{2,1,0:T(8,128)S(1)} %reduce_sum.81), channel_id=1, replica_groups=mesh['yl'=4,'c'=2,'x'=4,'yh'=2,'z'=8] {'x','yh','z'}, dimensions={0} | all-to-all | bytes 4194304 | tf_op jit(solution)/shard_map/all_to_all | solution.py:58
  82.1 1.7 reduce_sum.82
  83.8 0.7 broadcast_in_dim.31
  84.5 13.6 %all-to-all-start.2 = ((f32[8,8,1024]{2,1,0:T(8,128)}), f32[8,8,1024]{2,1,0:T(8,128)S(1)}, u32[]{:S(2)}, u32[]{:S(2)}) async-start(f32[8,8,1024]{2,1,0:T(8,128)} %broadcast_in_dim.31), calls=%async_computation.2 | async-start | bytes 524288 | tf_op jit(solution)/shard_map/all_to_all | solution.py:61
  98.1 8.7 %all-to-all-done.2 = f32[8,8,1024]{2,1,0:T(8,128)S(1)} async-done(((f32[8,8,1024]{2,1,0:T(8,128)}), f32[8,8,1024]{2,1,0:T(8,128)S(1)}, u32[]{:S(2)}, u32[]{:S(2)}) %all-to-all-start.2) | async-done | bytes 262176 | tf_op jit(solution)/shard_map/all_to_all | solution.py:61
  106.8 1.1 broadcast_in_dim.33
  107.9 4.8 %all-to-all-start.4 = ((bf16[64,8,1024]{2,1,0:T(8,128)(2,1)}), bf16[64,8,1024]{2,1,0:T(8,128)(2,1)S(1)}, u32[]{:S(2)}, u32[]{:S(2)}) async-start(bf16[64,8,1024]{2,1,0:T(8,128)(2,1)} %broadcast_in_dim.33), calls=%async_computation.4 | async-start | bytes 2097152 | tf_op jit(solution)/shard_map/all_to_all | solution.py:48
  112.8 30.1 %all-to-all-done.4 = bf16[64,8,1024]{2,1,0:T(8,128)(2,1)S(1)} async-done(((bf16[64,8,1024]{2,1,0:T(8,128)(2,1)}), bf16[64,8,1024]{2,1,0:T(8,128)(2,1)S(1)}, u32[]{:S(2)}, u32[]{:S(2)}) %all-to-all-start.4) | async-done | bytes 1048608 | tf_op jit(solution)/shard_map/all_to_all | solution.py:48
  142.9 1.1 broadcast_in_dim.32
  144.0 7.5 %all-to-all-start.3 = ((bf16[64,8,1024]{2,1,0:T(8,128)(2,1)}), bf16[64,8,1024]{2,1,0:T(8,128)(2,1)}, u32[]{:S(2)}, u32[]{:S(2)}) async-start(bf16[64,8,1024]{2,1,0:T(8,128)(2,1)} %broadcast_in_dim.32), calls=%async_computation.3 | async-start | bytes 2097152 | tf_op jit(solution)/shard_map/all_to_all | solution.py:73
  151.6 0.7 slice.65
  152.2 0.6 compare_reduce_fusion.1
  152.9 0.6 compare_reduce_fusion
  153.5 1.3 multiply_reduce_fusion
  154.8 20.6 %all-to-all-done.3 = bf16[64,8,1024]{2,1,0:T(8,128)(2,1)} async-done(((bf16[64,8,1024]{2,1,0:T(8,128)(2,1)}), bf16[64,8,1024]{2,1,0:T(8,128)(2,1)}, u32[]{:S(2)}, u32[]{:S(2)}) %all-to-all-start.3) | async-done | bytes 1048608 | tf_op jit(solution)/shard_map/all_to_all | solution.py:73
  175.4 1.5 pad_maximum_fusion
  176.9 0.5 broadcast_in_dim.34
  177.4 12.3 %all_to_all.47 = bf16[2,64,16,1024]{3,2,1,0:T(8,128)(2,1)S(1)} all-to-all(bf16[2,64,16,1024]{3,2,1,0:T(8,128)(2,1)S(1)} %broadcast_in_dim.34), channel_id=1, replica_groups=mesh['yl'=4,'c'=2,'x'=4,'yh'=2,'z'=8] {'c'}, dimensions={0} | all-to-all | bytes 8388608 | tf_op jit(solution)/shard_map/all_to_all | solution.py:74
  189.7 0.8 copy.35
  190.5 1.8 fusion.8
  192.3 2.9 %multiply_reduce_fusion.1 = (f32[]{:T(128)}, f32[16,1024]{1,0:T(8,128)S(1)}) fusion(bf16[1024,1024]{1,0:T(8,128)(2,1)} %bitcast.58, bf16[16,1024]{1,0:T(8,128)(2,1)S(1)} %copy-done.5, bf16[1024,1024]{1,0:T(8,128)(2,1)S(1)} %bitcast.50), kind=kOutput, calls=%fused_computation.19 | convolution fusion | flops 67158016 | bytes 4292612 | tf_op jit(solution)/shard_map/dot_general | solution.py:80
  196.5 2.5 fusion.10
  199.0 1.4 bitcast_dynamic-update-slice_fusion
  200.4 0.6 broadcast_in_dim.40
  201.0 10.0 %all-to-all-start.6 = ((f32[64,1,128]{2,1,0:T(1,128)}), f32[64,1,128]{2,1,0:T(1,128)S(1)}, u32[]{:S(2)}, u32[]{:S(2)}) async-start(f32[64,1,128]{2,1,0:T(1,128)} %broadcast_in_dim.40), calls=%async_computation.6 | async-start | bytes 65536 | tf_op jit(solution)/shard_map/all_to_all | solution.py:82
  211.0 13.1 %all-to-all-done.6 = f32[64,1,128]{2,1,0:T(1,128)S(1)} async-done(((f32[64,1,128]{2,1,0:T(1,128)}), f32[64,1,128]{2,1,0:T(1,128)S(1)}, u32[]{:S(2)}, u32[]{:S(2)}) %all-to-all-start.6) | async-done | bytes 32800 | tf_op jit(solution)/shard_map/all_to_all | solution.py:82
  224.1 0.7 slice_reduce_fusion
  226.3 0.6 copy-done.2
  227.0 1.1 broadcast_in_dim.82
  228.1 4.8 %all-to-all-start.7 = ((bf16[64,8,1024]{2,1,0:T(8,128)(2,1)}), bf16[64,8,1024]{2,1,0:T(8,128)(2,1)S(1)}, u32[]{:S(2)}, u32[]{:S(2)}) async-start(bf16[64,8,1024]{2,1,0:T(8,128)(2,1)} %broadcast_in_dim.82), calls=%async_computation.7 | async-start | bytes 2097152 | tf_op jit(solution)/shard_map/all_to_all | solution.py:89
  232.9 0.2 fusion.5
  233.1 0.7 fusion.9
  241.4 0.4 dynamic-slice_bitcast_fusion.3
  241.9 1.1 pad_maximum_fusion.1
  242.9 1.1 copy.29
  244.0 0.1 constant_dynamic-slice_fusion.3
  244.1 0.8 fusion.12
  244.8 0.1 copy-done.1
  244.9 1.2 fusion.2
  246.2 10.9 %all-to-all-done.7 = bf16[64,8,1024]{2,1,0:T(8,128)(2,1)S(1)} async-done(((bf16[64,8,1024]{2,1,0:T(8,128)(2,1)}), bf16[64,8,1024]{2,1,0:T(8,128)(2,1)S(1)}, u32[]{:S(2)}, u32[]{:S(2)}) %all-to-all-start.7) | async-done | bytes 1048608 | tf_op jit(solution)/shard_map/all_to_all | solution.py:89
  257.1 0.2 broadcast_in_dim.83
  257.4 10.1 %all_to_all.48 = bf16[2,64,8,1024]{3,2,1,0:T(8,128)(2,1)S(1)} all-to-all(bf16[2,64,8,1024]{3,2,1,0:T(8,128)(2,1)S(1)} %broadcast_in_dim.83), channel_id=1, replica_groups=mesh['yl'=4,'c'=2,'x'=4,'yh'=2,'z'=8] {'c'}, dimensions={0} | all-to-all | bytes 4194304 | tf_op jit(solution)/shard_map/all_to_all | solution.py:29
  267.5 1.5 copy.30
  (25 shorter events, 0.1 us)
Async XLA Ops:
  0.6 1.0 copy-start
  82.1 16.1 %copy-start.6 = (bf16[16,1024]{1,0:T(8,128)(2,1)S(1)}, bf16[16,1024]{1,0:T(8,128)(2,1)}, u32[]{:S(2)}) copy-start(bf16[16,1024]{1,0:T(8,128)(2,1)} %param.17) | copy-start | bytes 98308
  84.5 22.3 %all-to-all-start.2 = ((f32[8,8,1024]{2,1,0:T(8,128)}), f32[8,8,1024]{2,1,0:T(8,128)S(1)}, u32[]{:S(2)}, u32[]{:S(2)}) async-start(f32[8,8,1024]{2,1,0:T(8,128)} %broadcast_in_dim.31), calls=%async_computation.2 | async-start | bytes 524288 | tf_op jit(solution)/shard_map/all_to_all | solution.py:61
  107.9 35.0 %all-to-all-start.4 = ((bf16[64,8,1024]{2,1,0:T(8,128)(2,1)}), bf16[64,8,1024]{2,1,0:T(8,128)(2,1)S(1)}, u32[]{:S(2)}, u32[]{:S(2)}) async-start(bf16[64,8,1024]{2,1,0:T(8,128)(2,1)} %broadcast_in_dim.33), calls=%async_computation.4 | async-start | bytes 2097152 | tf_op jit(solution)/shard_map/all_to_all | solution.py:48
  112.7 40.8 %copy-start.3 = (f32[16,1024]{1,0:T(8,128)S(1)}, f32[16,1024]{1,0:T(8,128)}, u32[]{:S(2)}) copy-start(f32[16,1024]{1,0:T(8,128)} %param.15) | copy-start | bytes 196612
  144.0 31.4 %all-to-all-start.3 = ((bf16[64,8,1024]{2,1,0:T(8,128)(2,1)}), bf16[64,8,1024]{2,1,0:T(8,128)(2,1)}, u32[]{:S(2)}, u32[]{:S(2)}) async-start(bf16[64,8,1024]{2,1,0:T(8,128)(2,1)} %broadcast_in_dim.32), calls=%async_computation.3 | async-start | bytes 2097152 | tf_op jit(solution)/shard_map/all_to_all | solution.py:73
  190.5 1.8 copy-start.5
  192.3 34.0 %copy-start.4 = (f32[16,1024]{1,0:T(8,128)S(1)}, f32[16,1024]{1,0:T(8,128)}, u32[]{:S(2)}) copy-start(f32[16,1024]{1,0:T(8,128)} %param.14) | copy-start | bytes 196612
  195.2 37.7 %copy-start.7 = (s32[128]{0:T(128)S(1)}, s32[128]{0:T(128)}, u32[]{:S(2)}) copy-start(s32[128]{0:T(128)} %param.19) | copy-start | bytes 1540
  201.0 23.1 %all-to-all-start.6 = ((f32[64,1,128]{2,1,0:T(1,128)}), f32[64,1,128]{2,1,0:T(1,128)S(1)}, u32[]{:S(2)}, u32[]{:S(2)}) async-start(f32[64,1,128]{2,1,0:T(1,128)} %broadcast_in_dim.40), calls=%async_computation.6 | async-start | bytes 65536 | tf_op jit(solution)/shard_map/all_to_all | solution.py:82
  226.3 0.6 copy-start.2
  228.1 29.0 %all-to-all-start.7 = ((bf16[64,8,1024]{2,1,0:T(8,128)(2,1)}), bf16[64,8,1024]{2,1,0:T(8,128)(2,1)S(1)}, u32[]{:S(2)}, u32[]{:S(2)}) async-start(bf16[64,8,1024]{2,1,0:T(8,128)(2,1)} %broadcast_in_dim.82), calls=%async_computation.7 | async-start | bytes 2097152 | tf_op jit(solution)/shard_map/all_to_all | solution.py:89
  244.0 1.0 copy-start.1
